TPU v7x, 256 devices: a whole 4x4x8 slice. The times are simulated.
256 devices in a mesh: clu: 32 (over x, z), grp: 8 (over y, core).
Axes of the slice: x: 4, y: 4, z: 8, core: 2. Of those that a mesh axis runs over, the one named last changes fastest.
Arguments:
- tokens: bfloat16 [262144, 1024], P(('clu', 'grp')), may hold values from -6 to 6
- segment_ids: int32 [256, 1024], P(('clu', 'grp')), may hold values from 0 to 127, never falling along the last dimension, each value on 1 to 32 neighbouring positions
- w_in: bfloat16 [1024, 2048], replicated, may hold values from -0.1875 to 0.1875
- b_in: float32 [2048], replicated, may hold values from -4 to 4
- w_out: bfloat16 [2048, 1024], replicated, may hold values from -0.125 to 0.125
- b_out: float32 [1024], replicated, may hold values from -1.5 to 1.5
- owner_ids: int32 [32768, 1], P(('clu', 'grp')), may hold values from 0 to 31; in each aligned block of 128 rows (0 to 127, 128 to 255, ...) at most 8 rows name the same one
- sub_ids: int32 [32768], P(('clu', 'grp')), may hold values from 0 to 511
Outputs:
- pooled: bfloat16 [32768, 1024], P(('clu', 'grp'))
- nearest: float32 [32768], P(('clu', 'grp'))
Inputs may be any that keep to these rules, and one draw needn't show every extreme that they name: `owner_ids`: no device holds more than 8 documents of one owner; some device holds exactly 8. `segment_ids`: each row lists documents 0 to 127 in order, each on 1 to 32 consecutive positions, one on exactly 32.
All inputs are finite; a program needn't handle non-finite values.
Results may differ from a plain program's by a relative error of at most 0.0043.
Values may be sent and summed in bfloat16 or wider, within the bound.
No kernel may reach another device: no remote copies, remote signals or barrier semaphores. Data moves between devices by JAX's collectives and lax.ppermute only.
A program may use at most 64 MiB of HBM per device.

v0:
```python
import jax
import jax.numpy as jnp
from jax import lax
from jax.sharding import PartitionSpec as P


def encode(token_block, segments, w_in, b_in, w_out, b_out, doc_count):
    pre_act = jnp.dot(token_block, w_in, preferred_element_type=jnp.float32) + b_in
    activated = jax.nn.gelu(pre_act, approximate=False).astype(jnp.bfloat16)
    layer_out = (
        token_block.astype(jnp.float32)
        + jnp.dot(activated, w_out, preferred_element_type=jnp.float32)
        + b_out
    ).astype(jnp.bfloat16)
    member = segments[None, :] == jnp.arange(doc_count, dtype=jnp.int32)[:, None]
    totals = jnp.dot(member.astype(jnp.bfloat16), layer_out, preferred_element_type=jnp.float32)
    counts = jnp.sum(member.astype(jnp.float32), axis=1, keepdims=True)
    mean_rows = totals / counts
    scale_inv = lax.rsqrt(jnp.sum(mean_rows * mean_rows, axis=1, keepdims=True) + 1e-06)
    return (mean_rows.astype(jnp.bfloat16), (mean_rows * scale_inv).astype(jnp.bfloat16))


def absorb(best_sim, own_units, own_meta, piece_units, piece_meta):
    similar = lax.dot_general(
        own_units, piece_units, (((1,), (1,)), ((), ())), preferred_element_type=jnp.float32
    )
    own_key = own_meta[:, 1][:, None]
    matched = (
        (own_key == piece_meta[:, 1][None, :])
        & (own_key >= 0)
        & (own_meta[:, 0][:, None] != piece_meta[:, 0][None, :])
    )
    return jnp.maximum(best_sim, jnp.max(jnp.where(matched, similar, -1.0), axis=1))


def per_device(tokens, segment_ids, w_in, b_in, w_out, b_out, owner_ids, sub_ids):
    n_clu = lax.axis_size("clu")
    n_grp = lax.axis_size("grp")
    doc_count = owner_ids.shape[0]
    model_width = tokens.shape[1]
    capacity = 2 * doc_count // n_clu
    own_count = n_clu * capacity
    pooled, unit_rows = encode(tokens, segment_ids[0], w_in, b_in, w_out, b_out, doc_count)
    owner_rank = owner_ids[:, 0]
    owner_hits = (owner_rank[:, None] == jnp.arange(n_clu, dtype=jnp.int32)[None, :]).astype(
        jnp.int32
    )
    before = jnp.cumsum(owner_hits, axis=0) - owner_hits
    slot_index = jnp.sum(before * owner_hits, axis=1)
    slot_place = owner_rank * capacity + slot_index
    grp_index = lax.axis_index("grp")
    device_rank = lax.axis_index("clu") * n_grp + grp_index
    doc_index = device_rank * doc_count + jnp.arange(doc_count, dtype=jnp.int32)
    start_best = jnp.full((own_count,), -1.0, jnp.float32)
    doc_info = jnp.stack([slot_place, doc_index, sub_ids], axis=1)
    every_unit, every_info = (
        lax.all_gather(unit_rows, "grp", axis=0, tiled=True),
        lax.all_gather(doc_info, "grp", axis=0, tiled=True),
    )
    source_grp = jnp.arange(n_grp * doc_count, dtype=jnp.int32) // doc_count
    wide_place = (
        every_info[:, 0] // capacity * (n_grp * capacity)
        + source_grp * capacity
        + every_info[:, 0] % capacity
    )
    send_units = (
        jnp.zeros((n_clu * n_grp * capacity, model_width), jnp.bfloat16)
        .at[wide_place]
        .set(every_unit)
    )
    send_meta = (
        jnp.full((n_clu * n_grp * capacity, 2), -1, jnp.int32).at[wide_place].set(every_info[:, 1:])
    )
    got_units, got_meta = (
        lax.all_to_all(
            send_units.reshape(n_clu, n_grp * capacity, model_width),
            "clu",
            split_axis=0,
            concat_axis=0,
            tiled=True,
        ),
        lax.all_to_all(
            send_meta.reshape(n_clu, n_grp * capacity, 2),
            "clu",
            split_axis=0,
            concat_axis=0,
            tiled=True,
        ),
    )
    own_units = lax.dynamic_slice_in_dim(
        got_units.reshape(n_clu, n_grp, capacity, model_width), grp_index, 1, 1
    ).reshape(own_count, model_width)
    own_meta = lax.dynamic_slice_in_dim(
        got_meta.reshape(n_clu, n_grp, capacity, 2), grp_index, 1, 1
    ).reshape(own_count, 2)
    best_sim = absorb(
        start_best,
        own_units,
        own_meta,
        got_units.reshape(n_clu * n_grp * capacity, model_width),
        got_meta.reshape(n_clu * n_grp * capacity, 2),
    )
    returned = lax.all_to_all(
        best_sim.reshape(n_clu, capacity), "clu", split_axis=0, concat_axis=0, tiled=True
    )
    nearest = jnp.take(returned.reshape(own_count), slot_place)
    return (pooled, nearest)


def solution(mesh):
    in_specs = (
        P(("clu", "grp"), None),
        P(("clu", "grp"), None),
        P(),
        P(),
        P(),
        P(),
        P(("clu", "grp"), None),
        P(("clu", "grp")),
    )
    out_specs = (P(("clu", "grp"), None), P(("clu", "grp")))
    return jax.shard_map(
        per_device, mesh=mesh, in_specs=in_specs, out_specs=out_specs, check_vma=False
    )
```

profile of v0, /device:TPU:1, one launch (start us, length us, event | category | flops | bytes accessed | tf_op | source)
XLA Modules:
  0.0 217.7 jit_solution(3338972314123578086)
XLA Ops:
  7.2 0.0 all-gather.2.cloned.1.call-start
  7.2 0.8 convert_reduce_fusion
  8.0 0.0 copy-start
  8.0 0.0 copy-start.1
  8.0 0.0 copy-start.3
  8.1 30.1 %fusion.10 = f32[1024,1024]{1,0:T(8,128)} fusion(bf16[2048,1024]{1,0:T(8,128)(2,1)} %param.12, f32[2048]{0:T(1024)} %param.11, bf16[1024,1024]{1,0:T(8,128)(2,1)} %param.8, bf16[1024,2048]{1,0:T(8,128)(2,1)} %param.10), kind=kOutput, calls=%fused_computation.23 | convolution fusion | flops 8728346624 | bytes 14688256 | tf_op jit(solution)/shard_map/dot_general | solution.py:12
  38.2 0.0 copy-done
  38.2 0.0 copy-done.1
  38.2 0.0 copy-done.3
  38.2 0.0 copy-start.2
  38.2 0.0 copy-start.4
  38.2 3.1 %multiply_reduce_fusion = (f32[128]{0:T(128)S(1)}, f32[128,1024]{1,0:T(8,128)S(1)}) fusion(f32[128]{0:T(128)S(1)} %convert_reduce_fusion, f32[1024,1024]{1,0:T(8,128)} %fusion.10, bf16[1024,1024]{1,0:T(8,128)(2,1)S(1)} %copy-done, f32[1024]{0:T(1024)S(1)} %copy-done.3, s32[1024]{0:T(1024)S(1)} %bitcast.43), kind=kOutput, calls=%fused_computation.35 | convolution fusion | flops 273153920 | bytes 6824960 | tf_op jit(solution)/shard_map/dot_general | solution.py:16
  41.3 0.8 multiply_convert_fusion
  42.1 0.0 all-gather.2.cloned.1.call-update
  42.2 0.0 copy-done.2
  42.2 0.1 fusion.25
  42.3 0.2 reduce_window_sum.11
  42.4 0.2 select_reduce_fusion
  42.6 0.0 copy-done.4
  42.6 14.5 %all_gather.6 = s32[1024,3]{0,1:T(4,128)S(1)} all-gather(s32[128,3]{0,1:T(4,128)S(1)} %pad_add_fusion), channel_id=1, replica_groups=mesh['clu'=32,'grp'=8] {'grp'}, dimensions={0}, use_global_device_ids=true | all-gather | bytes 13824 | tf_op jit(solution)/shard_map/all_gather | solution.py:58
  57.2 0.2 copy.28
  57.5 3.3 %scatter_custom_fusion = s32[2048,2]{1,0:T(8,128)S(1)} fusion(s32[1024]{0:T(1024)S(1)} %bitcast.48, s32[1024,2]{1,0:T(8,128)S(1)} %copy.28, s32[]{:T(128)} %constant.133.clone.1), kind=kCustom, calls=%fused_computation.36 | custom fusion | bytes 16388 | tf_op jit(solution)/shard_map/scatter | solution.py:72
  60.8 0.4 copy.29
  61.2 0.7 reshape.157
  61.9 10.2 %all-to-all-start = ((s32[32,1,128]{2,1,0:T(1,128)}), s32[32,1,128]{2,1,0:T(1,128)S(1)}, u32[]{:S(2)}, u32[]{:S(2)}) async-start(s32[32,1,128]{2,1,0:T(1,128)} %reshape.157), calls=%async_computation | async-start | bytes 32768 | tf_op jit(solution)/shard_map/all_to_all | solution.py:82
  72.2 2.2 %all-gather.2.cloned.1.call-done = bf16[1024,1024]{1,0:T(8,128)(2,1)} async-done(((bf16[128,1024]{1,0:T(8,128)(2,1)}), bf16[1024,1024]{1,0:T(8,128)(2,1)}) %all-gather.2.cloned.1.call-update) | async-done | bytes 2097168 | tf_op jit(solution)/shard_map/all_gather | solution.py:57
  74.4 8.6 %scatter_custom_fusion.1 = bf16[2048,1024]{1,0:T(8,128)(2,1)} fusion(s32[1024]{0:T(1024)S(1)} %bitcast.49, bf16[1024,1024]{1,0:T(8,128)(2,1)} %all-gather.2.cloned.1.call-done, bf16[]{:T(256)} %constant.144.clone.1), kind=kCustom, calls=%fused_computation.27 | custom fusion | bytes 4194816 | tf_op jit(solution)/shard_map/scatter | solution.py:69
  82.9 0.0 all-to-all-done
  82.9 9.7 %all-to-all-start.1 = ((bf16[32,64,1024]{2,1,0:T(8,128)(2,1)}), bf16[32,64,1024]{2,1,0:T(8,128)(2,1)}, u32[]{:S(2)}, u32[]{:S(2)}) async-start(bf16[32,64,1024]{2,1,0:T(8,128)(2,1)} %bitcast.36), calls=%async_computation.1 | async-start | bytes 8388608 | tf_op jit(solution)/shard_map/all_to_all | solution.py:75
  92.6 0.5 broadcast.140
  93.1 0.7 reduce.6
  93.8 0.1 reshape.158
  93.9 0.1 copy.30
  94.0 0.1 copy.31
  94.1 0.1 reshape.112
  94.2 0.1 reshape.113
  94.3 92.6 %all-to-all-done.1 = bf16[32,64,1024]{2,1,0:T(8,128)(2,1)} async-done(((bf16[32,64,1024]{2,1,0:T(8,128)(2,1)}), bf16[32,64,1024]{2,1,0:T(8,128)(2,1)}, u32[]{:S(2)}, u32[]{:S(2)}) %all-to-all-start.1) | async-done | bytes 4194336 | tf_op jit(solution)/shard_map/all_to_all | solution.py:75
  186.9 4.0 %fusion.18 = f32[256]{0:T(256)S(1)} fusion(bf16[2048,1024]{1,0:T(8,128)(2,1)} %bitcast.15, s32[2048]{0:T(1024)S(1)} %bitcast.45, s32[2048]{0:T(1024)S(1)} %bitcast.44, s32[256]{0:T(256)S(1)} %bitcast.51, s32[256]{0:T(256)S(1)} %bitcast.50, pred[256]{0:T(512)(128)(4,1)S(1)} %compare_reduce_fusion, bf16[32,8,8,1024]{3,2,1,0:T(8,128)(2,1)} %bitcast.13, ...), kind=kOutput, calls=%fused_computation.30 | convolution fusion | flops 1076887296 | bytes 4738308 | tf_op jit(solution)/shard_map/dot_general | solution.py:24
  190.9 0.7 max_broadcast_in_dim.15
  191.6 7.5 %all-to-all-start.2 = ((f32[32,1,8]{2,1,0:T(1,128)}), f32[32,1,8]{2,1,0:T(1,128)S(1)}, u32[]{:S(2)}, u32[]{:S(2)}) async-start(f32[32,1,8]{2,1,0:T(1,128)} %bitcast.16), calls=%async_computation.2 | async-start | bytes 32768 | tf_op jit(solution)/shard_map/all_to_all | solution.py:103
  199.2 8.6 %all-to-all-done.2 = f32[32,1,8]{2,1,0:T(1,128)S(1)} async-done(((f32[32,1,8]{2,1,0:T(1,128)}), f32[32,1,8]{2,1,0:T(1,128)S(1)}, u32[]{:S(2)}, u32[]{:S(2)}) %all-to-all-start.2) | async-done | bytes 1056 | tf_op jit(solution)/shard_map/all_to_all | solution.py:103
  207.8 0.5 broadcast.139
  208.3 0.7 reduce.5
  209.0 0.1 reshape.118
  209.1 1.3 gather_fusion
  210.4 0.5 bitcast_select_fusion
  (12 shorter events, 0.1 us)
Async XLA Ops:
  7.2 67.2 %all-gather.2.cloned.1.call-start = ((), (), s32[]{:S(2)}) async-start(), calls=%async_computation.3 | async-start | bytes 2359296 | tf_op jit(solution)/shard_map/all_gather | solution.py:57
  8.0 30.1 %copy-start = (bf16[1024,1024]{1,0:T(8,128)(2,1)S(1)}, bf16[1024,1024]{1,0:T(8,128)(2,1)}, u32[]{:S(2)}) copy-start(bf16[1024,1024]{1,0:T(8,128)(2,1)} %param.8) | copy-start | bytes 6291460
  8.0 30.1 %copy-start.1 = (s32[1,1024]{1,0:T(1,128)S(1)}, s32[1,1024]{1,0:T(1,128)}, u32[]{:S(2)}) copy-start(s32[1,1024]{1,0:T(1,128)} %param.9) | copy-start | bytes 12292
  8.0 30.1 %copy-start.3 = (f32[1024]{0:T(1024)S(1)}, f32[1024]{0:T(1024)}, u32[]{:S(2)}) copy-start(f32[1024]{0:T(1024)} %param.13) | copy-start | bytes 12292
  38.2 4.0 %copy-start.2 = (s32[128,1]{0,1:T(1,128)S(1)}, s32[128,1]{0,1:T(1,128)}, u32[]{:S(2)}) copy-start(s32[128,1]{0,1:T(1,128)} %param.14) | copy-start | bytes 1540
  38.2 4.4 %copy-start.4 = (s32[128]{0:T(128)S(1)}, s32[128]{0:T(128)}, u32[]{:S(2)}) copy-start(s32[128]{0:T(128)} %param.15) | copy-start | bytes 1540
  61.9 21.0 %all-to-all-start = ((s32[32,1,128]{2,1,0:T(1,128)}), s32[32,1,128]{2,1,0:T(1,128)S(1)}, u32[]{:S(2)}, u32[]{:S(2)}) async-start(s32[32,1,128]{2,1,0:T(1,128)} %reshape.157), calls=%async_computation | async-start | bytes 32768 | tf_op jit(solution)/shard_map/all_to_all | solution.py:82
  82.9 104.0 %all-to-all-start.1 = ((bf16[32,64,1024]{2,1,0:T(8,128)(2,1)}), bf16[32,64,1024]{2,1,0:T(8,128)(2,1)}, u32[]{:S(2)}, u32[]{:S(2)}) async-start(bf16[32,64,1024]{2,1,0:T(8,128)(2,1)} %bitcast.36), calls=%async_computation.1 | async-start | bytes 8388608 | tf_op jit(solution)/shard_map/all_to_all | solution.py:75
  191.6 16.2 %all-to-all-start.2 = ((f32[32,1,8]{2,1,0:T(1,128)}), f32[32,1,8]{2,1,0:T(1,128)S(1)}, u32[]{:S(2)}, u32[]{:S(2)}) async-start(f32[32,1,8]{2,1,0:T(1,128)} %bitcast.16), calls=%async_computation.2 | async-start | bytes 32768 | tf_op jit(solution)/shard_map/all_to_all | solution.py:103
Sparse Core Ops, SparseCore 0:
  42.3 32.0 all-gather.1
where the time goes:
time: 218 us
  waiting for transfers between devices  103 us (47%)
  matrix products  37.2 us (17%)
  starting transfers between devices  27.5 us (13%)
  local copies, waits for them, and re-layouts  16.8 us (8%)
  blocking collectives  14.5 us (7%)
  between operations  14.2 us (7%)
  other arithmetic  4.08 us (2%)
    all_to_all x1, waiting for transfers between devices, per_device(): lax.all_to_all(send_units.reshape(n_clu, n_grp * capacity, model_width),...  92.6 us
    dot_general x1, matrix products, encode(): jnp.dot(activated, w_out, preferred_element_type=jnp.float32)  30.1 us
    all_gather x1, blocking collectives, per_device(): lax.all_gather(doc_info, 'grp', axis=0, tiled=True)  14.5 us
    all_to_all x1, starting transfers between devices, per_device(): lax.all_to_all(send_meta.reshape(n_clu, n_grp * capacity, 2), 'clu', spli...  10.2 us
    all_to_all x1, starting transfers between devices, per_device(): lax.all_to_all(send_units.reshape(n_clu, n_grp * capacity, model_width),...  9.67 us
    all_to_all x1, waiting for transfers between devices, per_device(): lax.all_to_all(best_sim.reshape(n_clu, capacity), 'clu', split_axis=0, co...  8.64 us
    scatter x1, local copies, waits for them, and re-layouts, per_device(): send_units = jnp.zeros((n_clu * n_grp * capacity, model_width), jnp.bfloa...  8.55 us
    all_to_all x1, starting transfers between devices, per_device(): lax.all_to_all(best_sim.reshape(n_clu, capacity), 'clu', split_axis=0, co...  7.54 us
  transfers between devices with their start and end apart: 4, of which 3 were waited for; matrix products, arithmetic and copies ran while one was open for 7% of the time, Pallas kernels for 0%

commit v1 on v0

--- a/solution.py
+++ b/solution.py
@@ -55,7 +55,9 @@
     doc_info = jnp.stack([slot_place, doc_index, sub_ids], axis=1)
     every_unit, every_info = (
         lax.all_gather(unit_rows, "grp", axis=0, tiled=True),
-        lax.all_gather(doc_info, "grp", axis=0, tiled=True),
+        jnp.concatenate(
+            lax.all_to_all(jnp.stack([doc_info] * lax.axis_size("grp")), "grp", 0, 0), axis=0
+        ),
     )
     source_grp = jnp.arange(n_grp * doc_count, dtype=jnp.int32) // doc_count
     wide_place = (

time: 218 us -> 218 us (level)
  blocking collectives: 14.5 us -> 10.4 us
  waiting for transfers between devices: 103 us -> 107 us
    all_gather x1 -> x0, blocking collectives: 14.5 us -> none  [per_device(): lax.all_gather(doc_info, 'grp', axis=0, tiled=True)]
    all_to_all x0 -> x1, blocking collectives: none -> 10.4 us  [per_device(): lax.all_to_all(jnp.stack([doc_info] * lax.axis_size('grp')), 'grp', 0, 0)]
    all_gather x1, waiting for transfers between devices: 2.2 us -> 5.52 us  [per_device(): lax.all_gather(unit_rows, 'grp', axis=0, tiled=True)]
where the time goes in v1:
time: 218 us
  waiting for transfers between devices  107 us (49%)
  matrix products  37.2 us (17%)
  starting transfers between devices  28.3 us (13%)
  local copies, waits for them, and re-layouts  16.8 us (8%)
  between operations  14.2 us (7%)
  blocking collectives  10.4 us (5%)
  other arithmetic  4.08 us (2%)
    all_to_all x1, waiting for transfers between devices, per_device(): lax.all_to_all(send_units.reshape(n_clu, n_grp * capacity, model_width),...  92.6 us
    dot_general x1, matrix products, encode(): jnp.dot(activated, w_out, preferred_element_type=jnp.float32)  30.1 us
    all_to_all x1, starting transfers between devices, per_device(): lax.all_to_all(send_meta.reshape(n_clu, n_grp * capacity, 2), 'clu', spli...  11 us
    all_to_all x1, blocking collectives, per_device(): lax.all_to_all(jnp.stack([doc_info] * lax.axis_size('grp')), 'grp', 0, 0)  10.4 us
    all_to_all x1, starting transfers between devices, per_device(): lax.all_to_all(send_units.reshape(n_clu, n_grp * capacity, model_width),...  9.67 us
    all_to_all x1, waiting for transfers between devices, per_device(): lax.all_to_all(best_sim.reshape(n_clu, capacity), 'clu', split_axis=0, co...  8.64 us
    scatter x1, local copies, waits for them, and re-layouts, per_device(): send_units = jnp.zeros((n_clu * n_grp * capacity, model_width), jnp.bfloa...  8.55 us
    all_to_all x1, starting transfers between devices, per_device(): lax.all_to_all(best_sim.reshape(n_clu, capacity), 'clu', split_axis=0, co...  7.53 us
  transfers between devices with their start and end apart: 4, of which 3 were waited for; matrix products, arithmetic and copies ran while one was open for 7% of the time, Pallas kernels for 0%

profile of v1, /device:TPU:1, one launch (start us, length us, event | category | flops | bytes accessed | tf_op | source)
XLA Modules:
  0.0 217.7 jit_solution(15635832240464519657)
XLA Ops:
  7.2 0.0 all-gather.2.cloned.1.call-start
  7.2 0.8 convert_reduce_fusion
  8.0 0.0 copy-start
  8.0 0.0 copy-start.1
  8.0 0.0 copy-start.3
  8.1 30.1 %fusion.10 = f32[1024,1024]{1,0:T(8,128)} fusion(bf16[2048,1024]{1,0:T(8,128)(2,1)} %param.12, f32[2048]{0:T(1024)} %param.11, bf16[1024,1024]{1,0:T(8,128)(2,1)} %param.8, bf16[1024,2048]{1,0:T(8,128)(2,1)} %param.10), kind=kOutput, calls=%fused_computation.23 | convolution fusion | flops 8728346624 | bytes 14688256 | tf_op jit(solution)/shard_map/dot_general | solution.py:12
  38.2 0.0 copy-done
  38.2 0.0 copy-done.1
  38.2 0.0 copy-done.3
  38.2 0.0 copy-start.2
  38.2 0.0 copy-start.4
  38.2 3.1 %multiply_reduce_fusion = (f32[128]{0:T(128)S(1)}, f32[128,1024]{1,0:T(8,128)S(1)}) fusion(f32[128]{0:T(128)S(1)} %convert_reduce_fusion, f32[1024,1024]{1,0:T(8,128)} %fusion.10, bf16[1024,1024]{1,0:T(8,128)(2,1)S(1)} %copy-done, f32[1024]{0:T(1024)S(1)} %copy-done.3, s32[1024]{0:T(1024)S(1)} %bitcast.46), kind=kOutput, calls=%fused_computation.35 | convolution fusion | flops 273153920 | bytes 6824960 | tf_op jit(solution)/shard_map/dot_general | solution.py:16
  41.3 0.8 multiply_convert_fusion
  42.1 0.0 all-gather.2.cloned.1.call-update
  42.2 0.0 copy-done.2
  42.2 0.1 fusion.25
  42.3 0.2 reduce_window_sum.11
  42.4 0.2 select_reduce_fusion
  42.6 0.0 copy-done.4
  42.7 10.4 %all_to_all.21 = s32[8,128,3]{1,2,0:T(4,128)S(1)} all-to-all(s32[8,128,3]{1,2,0:T(4,128)S(1)} %stack.8), channel_id=1, replica_groups=mesh['clu'=32,'grp'=8] {'grp'}, dimensions={0} | all-to-all | bytes 24576 | tf_op jit(solution)/shard_map/all_to_all | solution.py:59
  53.1 0.2 copy.25
  53.4 3.3 %scatter_custom_fusion = s32[2048,2]{1,0:T(8,128)S(1)} fusion(s32[1024]{0:T(1024)S(1)} %bitcast.51, s32[1024,2]{1,0:T(8,128)S(1)} %copy.25, s32[]{:T(128)} %constant.133.clone.1), kind=kCustom, calls=%fused_computation.36 | custom fusion | bytes 16388 | tf_op jit(solution)/shard_map/scatter | solution.py:74
  56.7 0.4 copy.26
  57.1 0.7 reshape.163
  57.8 11.0 %all-to-all-start.1 = ((s32[32,1,128]{2,1,0:T(1,128)}), s32[32,1,128]{2,1,0:T(1,128)S(1)}, u32[]{:S(2)}, u32[]{:S(2)}) async-start(s32[32,1,128]{2,1,0:T(1,128)} %reshape.163), calls=%async_computation.1 | async-start | bytes 32768 | tf_op jit(solution)/shard_map/all_to_all | solution.py:84
  68.8 5.5 %all-gather.2.cloned.1.call-done = bf16[1024,1024]{1,0:T(8,128)(2,1)} async-done(((bf16[128,1024]{1,0:T(8,128)(2,1)}), bf16[1024,1024]{1,0:T(8,128)(2,1)}) %all-gather.2.cloned.1.call-update) | async-done | bytes 2097168 | tf_op jit(solution)/shard_map/all_gather | solution.py:57
  74.4 8.6 %scatter_custom_fusion.1 = bf16[2048,1024]{1,0:T(8,128)(2,1)} fusion(s32[1024]{0:T(1024)S(1)} %bitcast.52, bf16[1024,1024]{1,0:T(8,128)(2,1)} %all-gather.2.cloned.1.call-done, bf16[]{:T(256)} %constant.144.clone.1), kind=kCustom, calls=%fused_computation.27 | custom fusion | bytes 4194816 | tf_op jit(solution)/shard_map/scatter | solution.py:71
  82.9 0.0 all-to-all-done.1
  82.9 9.7 %all-to-all-start.2 = ((bf16[32,64,1024]{2,1,0:T(8,128)(2,1)}), bf16[32,64,1024]{2,1,0:T(8,128)(2,1)}, u32[]{:S(2)}, u32[]{:S(2)}) async-start(bf16[32,64,1024]{2,1,0:T(8,128)(2,1)} %bitcast.37), calls=%async_computation.2 | async-start | bytes 8388608 | tf_op jit(solution)/shard_map/all_to_all | solution.py:77
  92.6 0.5 broadcast.142
  93.1 0.7 reduce.6
  93.8 0.1 reshape.164
  93.9 0.1 copy.27
  94.0 0.1 copy.28
  94.1 0.1 reshape.118
  94.2 0.1 reshape.119
  94.3 92.6 %all-to-all-done.2 = bf16[32,64,1024]{2,1,0:T(8,128)(2,1)} async-done(((bf16[32,64,1024]{2,1,0:T(8,128)(2,1)}), bf16[32,64,1024]{2,1,0:T(8,128)(2,1)}, u32[]{:S(2)}, u32[]{:S(2)}) %all-to-all-start.2) | async-done | bytes 4194336 | tf_op jit(solution)/shard_map/all_to_all | solution.py:77
  186.9 4.0 %fusion.18 = f32[256]{0:T(256)S(1)} fusion(bf16[2048,1024]{1,0:T(8,128)(2,1)} %bitcast.16, s32[2048]{0:T(1024)S(1)} %bitcast.48, s32[2048]{0:T(1024)S(1)} %bitcast.47, s32[256]{0:T(256)S(1)} %bitcast.54, s32[256]{0:T(256)S(1)} %bitcast.53, pred[256]{0:T(512)(128)(4,1)S(1)} %compare_reduce_fusion, bf16[32,8,8,1024]{3,2,1,0:T(8,128)(2,1)} %bitcast.14, ...), kind=kOutput, calls=%fused_computation.30 | convolution fusion | flops 1076887296 | bytes 4738308 | tf_op jit(solution)/shard_map/dot_general | solution.py:24
  190.9 0.7 max_broadcast_in_dim.15
  191.6 7.5 %all-to-all-start.3 = ((f32[32,1,8]{2,1,0:T(1,128)}), f32[32,1,8]{2,1,0:T(1,128)S(1)}, u32[]{:S(2)}, u32[]{:S(2)}) async-start(f32[32,1,8]{2,1,0:T(1,128)} %bitcast.17), calls=%async_computation.3 | async-start | bytes 32768 | tf_op jit(solution)/shard_map/all_to_all | solution.py:105
  199.2 8.6 %all-to-all-done.3 = f32[32,1,8]{2,1,0:T(1,128)S(1)} async-done(((f32[32,1,8]{2,1,0:T(1,128)}), f32[32,1,8]{2,1,0:T(1,128)S(1)}, u32[]{:S(2)}, u32[]{:S(2)}) %all-to-all-start.3) | async-done | bytes 1056 | tf_op jit(solution)/shard_map/all_to_all | solution.py:105
  207.8 0.5 broadcast.141
  208.3 0.7 reduce.5
  209.0 0.1 reshape.124
  209.1 1.3 gather_fusion
  210.4 0.5 bitcast_select_fusion
  (13 shorter events, 0.1 us)
Async XLA Ops:
  7.2 67.2 %all-gather.2.cloned.1.call-start = ((), (), s32[]{:S(2)}) async-start(), calls=%async_computation.4 | async-start | bytes 2359296 | tf_op jit(solution)/shard_map/all_gather | solution.py:57
  8.0 30.1 %copy-start = (bf16[1024,1024]{1,0:T(8,128)(2,1)S(1)}, bf16[1024,1024]{1,0:T(8,128)(2,1)}, u32[]{:S(2)}) copy-start(bf16[1024,1024]{1,0:T(8,128)(2,1)} %param.8) | copy-start | bytes 6291460
  8.0 30.1 %copy-start.1 = (s32[1,1024]{1,0:T(1,128)S(1)}, s32[1,1024]{1,0:T(1,128)}, u32[]{:S(2)}) copy-start(s32[1,1024]{1,0:T(1,128)} %param.9) | copy-start | bytes 12292
  8.0 30.1 %copy-start.3 = (f32[1024]{0:T(1024)S(1)}, f32[1024]{0:T(1024)}, u32[]{:S(2)}) copy-start(f32[1024]{0:T(1024)} %param.13) | copy-start | bytes 12292
  38.2 4.0 %copy-start.2 = (s32[128,1]{0,1:T(1,128)S(1)}, s32[128,1]{0,1:T(1,128)}, u32[]{:S(2)}) copy-start(s32[128,1]{0,1:T(1,128)} %param.14) | copy-start | bytes 1540
  38.2 4.4 %copy-start.4 = (s32[128]{0:T(128)S(1)}, s32[128]{0:T(128)}, u32[]{:S(2)}) copy-start(s32[128]{0:T(128)} %param.15) | copy-start | bytes 1540
  57.8 25.1 %all-to-all-start.1 = ((s32[32,1,128]{2,1,0:T(1,128)}), s32[32,1,128]{2,1,0:T(1,128)S(1)}, u32[]{:S(2)}, u32[]{:S(2)}) async-start(s32[32,1,128]{2,1,0:T(1,128)} %reshape.163), calls=%async_computation.1 | async-start | bytes 32768 | tf_op jit(solution)/shard_map/all_to_all | solution.py:84
  82.9 104.0 %all-to-all-start.2 = ((bf16[32,64,1024]{2,1,0:T(8,128)(2,1)}), bf16[32,64,1024]{2,1,0:T(8,128)(2,1)}, u32[]{:S(2)}, u32[]{:S(2)}) async-start(bf16[32,64,1024]{2,1,0:T(8,128)(2,1)} %bitcast.37), calls=%async_computation.2 | async-start | bytes 8388608 | tf_op jit(solution)/shard_map/all_to_all | solution.py:77
  191.6 16.2 %all-to-all-start.3 = ((f32[32,1,8]{2,1,0:T(1,128)}), f32[32,1,8]{2,1,0:T(1,128)S(1)}, u32[]{:S(2)}, u32[]{:S(2)}) async-start(f32[32,1,8]{2,1,0:T(1,128)} %bitcast.17), calls=%async_computation.3 | async-start | bytes 32768 | tf_op jit(solution)/shard_map/all_to_all | solution.py:105
Sparse Core Ops, SparseCore 0:
  42.3 32.0 all-gather.1
